TPU v7x, 512 devices: a whole 4x4x16 slice. The times are simulated.
512 devices in a mesh: dp: 32 (over y, x, core), wide: 16 (over z).
Axes of the slice: x: 4, y: 4, z: 16, core: 2. Of those that a mesh axis runs over, the one named last changes fastest.
Arguments:
- trunk_out: bfloat16 [16384, 1024], P('dp'), may hold values from -6 to 6
- projection: bfloat16 [1024, 4096], P(None, 'wide'), may hold values from -0.1875 to 0.1875
- transform: bfloat16 [4096, 4096], P('wide'), may hold values from -0.125 to 0.125
- block_mask: int32 [32, 32], P('wide'), may hold values from 0 to 1, as said below
- old_index: bfloat16 [16384, 4096], P('dp', 'wide'), may hold values from -6 to 6
- doc_ids: int32 [16384, 4], P('dp'), may hold values from 0 to 16383, as said below
- labels: int32 [16384, 4], P('dp'), may hold values 0 or 1
Outputs:
- new_embed: bfloat16 [16384, 4096], P('dp', 'wide')
- pair_loss: float32 [16384, 4], P('dp')
- trunk_grad: bfloat16 [16384, 4096], P('dp', 'wide')
Inputs may be any that keep to these rules, and one draw needn't show every extreme that they name: `doc_ids`: in each aligned block of 512 rows, no shard id // 512 is named more than 128 times, and one shard is named exactly 128 times. `block_mask`: each block row has 4 to 24 nonzero entries, and some block row has exactly 24.
All inputs are finite; a program needn't handle non-finite values. No bound on the sum of `labels` on one device may be relied on, other than what follows from the above.
Results may differ from a plain program's by a relative error of at most 0.015.
Values may be sent and summed in bfloat16 or wider, within the bound.
No kernel may reach another device: no remote copies, remote signals or barrier semaphores. Data moves between devices by JAX's collectives and lax.ppermute only.
A program may use at most 128 MiB of HBM per device.

v0:
```python
import math
import jax
import jax.numpy as jnp
from jax import lax
from jax.sharding import PartitionSpec as P

E = 4096
K = 4
CAP = 128


def local(n_dp, trunk_out, projection, transform, block_mask, old_index, doc_ids, labels):
    rows, dmodel = trunk_out.shape
    e_local, width = transform.shape
    local_blocks, nblocks = block_mask.shape
    side = e_local // local_blocks
    doc_shard = old_index.shape[0]
    blocks = transform.reshape(local_blocks, side, nblocks, side)
    masked = (blocks * block_mask[:, None, :, None].astype(jnp.bfloat16)).reshape(e_local, width)
    chunk = dmodel // n_dp
    me = lax.axis_index("dp")
    proj_rows = lax.dynamic_slice_in_dim(projection, me * chunk, chunk, 0)
    w_part = jnp.dot(proj_rows, masked, preferred_element_type=jnp.float32)
    w_blk = lax.psum_scatter(w_part, "wide", scatter_dimension=1, tiled=True)
    w_cols = lax.all_gather(w_blk.astype(jnp.bfloat16), "dp", axis=0, tiled=True)
    new = jnp.dot(trunk_out, w_cols, preferred_element_type=jnp.float32)
    flat = doc_ids.reshape(-1)
    owner = flat // doc_shard
    loc = flat - owner * doc_shard
    onehot = (owner[:, None] == jnp.arange(n_dp, dtype=jnp.int32)[None, :]).astype(jnp.int32)
    before = jnp.cumsum(onehot, axis=0) - onehot
    rank = jnp.sum(before * onehot, axis=1)
    slot = owner * CAP + rank
    req = jnp.zeros((n_dp * CAP,), jnp.int32).at[slot].set(loc, unique_indices=True)
    asked = lax.all_to_all(req.reshape(n_dp, CAP), "dp", 0, 0, tiled=True)
    served = old_index[asked.reshape(-1)].reshape(n_dp, CAP, e_local)
    back = lax.all_to_all(served, "dp", 0, 0, tiled=True).reshape(n_dp * CAP, e_local)
    old_vec = back[slot].reshape(rows, K, e_local)
    old_wide = old_vec.astype(jnp.float32)
    scale = 1.0 / math.sqrt(E)
    partial_scores = jnp.einsum("re,rke->rk", new, old_wide)
    score = lax.psum(partial_scores, "wide") * scale
    sign = 2.0 * labels.astype(jnp.float32) - 1.0
    pair_loss = jax.nn.softplus(-sign * score)
    dscore = -sign * jax.nn.sigmoid(-sign * score)
    grad_local = (jnp.einsum("rk,rke->re", dscore, old_wide) * scale).astype(jnp.bfloat16)
    grad_full = lax.all_gather(grad_local, "wide", axis=1, tiled=True)
    trunk_grad = lax.dot_general(
        grad_full, masked, (((1,), (1,)), ((), ())), preferred_element_type=jnp.float32
    )
    return (new.astype(jnp.bfloat16), pair_loss, trunk_grad.astype(jnp.bfloat16))


def solution(mesh):
    n_dp = mesh.shape["dp"]
    return jax.shard_map(
        lambda *a: local(n_dp, *a),
        mesh=mesh,
        in_specs=(
            P("dp", None),
            P(None, "wide"),
            P("wide", None),
            P("wide", None),
            P("dp", "wide"),
            P("dp", None),
            P("dp", None),
        ),
        out_specs=(P("dp", "wide"), P("dp", None), P("dp", "wide")),
        check_vma=False,
    )
```

profile of v0, /device:TPU:2, one launch (start us, length us, event | category | flops | bytes accessed | tf_op | source)
XLA Modules:
  0.0 318.5 jit_solution(10625858685940429330)
XLA Ops:
  7.2 0.9 copy.11
  8.7 9.1 %reduce-window.6 = s32[32,16,128]{2,1,0:T(8,128)S(1)} reduce-window(s32[32,16,128]{2,1,0:T(8,128)S(1)} %fusion.5, s32[]{:T(128)} %constant.20.clone.1), window={size=1x1x128 pad=0_0x0_0x127_0}, to_apply=%region_1.2 | reduce-window | flops 8323072 | bytes 524292 | tf_op jit(solution)/shard_map/reduce-window
  18.7 8.1 %scatter_custom_fusion = s32[4096]{0:T(1024)S(1)} fusion(s32[2048]{0:T(1024)S(1)} %bitcast.60, s32[2048]{0:T(1024)S(1)} %get-tuple-element.9, s32[]{:T(128)} %constant.20.clone.1), kind=kCustom, calls=%fused_computation.42 | custom fusion | bytes 16388 | tf_op jit(solution)/shard_map/scatter | solution.py:34
  26.7 14.8 %all_to_all.14 = s32[32,1,128]{2,1,0:T(1,128)S(1)} all-to-all(s32[32,1,128]{2,1,0:T(1,128)S(1)} %bitcast.57), channel_id=1, replica_groups=mesh['dp'=32,'wide'=16] {'dp'}, dimensions={0} | all-to-all | bytes 32768 | tf_op jit(solution)/shard_map/all_to_all | solution.py:35
  41.6 16.9 %gather_fusion = bf16[4096,256]{1,0:T(8,128)(2,1)} fusion(bf16[512,256]{1,0:T(8,128)(2,1)S(1)} %copy-done.1, s32[4096]{0:T(1024)S(1)} %broadcast_clamp_fusion), kind=kCustom, calls=%fused_computation | custom fusion | bytes 4210688 | tf_op jit(solution)/shard_map/gather | solution.py:36
  58.5 5.2 %all-to-all-start.1 = ((bf16[32,128,256]{2,1,0:T(8,128)(2,1)}), bf16[32,128,256]{2,1,0:T(8,128)(2,1)S(1)}, u32[]{:S(2)}, u32[]{:S(2)}) async-start(bf16[32,128,256]{2,1,0:T(8,128)(2,1)} %bitcast.53), calls=%async_computation.2 | async-start | bytes 4194304 | tf_op jit(solution)/shard_map/all_to_all | solution.py:37
  64.2 1.3 copy-done.2
  66.1 2.4 fusion
  68.5 72.4 %reduce-scatter.2.cloned.1.call-done = f32[32,256]{1,0:T(8,128)} async-done(((f32[32,4096]{1,0:T(8,128)}), f32[32,256]{1,0:T(8,128)}) %reduce-scatter.2.cloned.1.call-update) | async-done | bytes 32784 | tf_op jit(solution)/shard_map/reduce_scatter | solution.py:24
  140.9 0.8 convert_element_type.28
  141.7 24.5 %all_gather.6 = bf16[1024,256]{1,0:T(8,128)(2,1)S(1)} all-gather(bf16[32,256]{1,0:T(8,128)(2,1)S(1)} %convert_element_type.28), channel_id=1, replica_groups=mesh['dp'=32,'wide'=16] {'dp'}, dimensions={0}, use_global_device_ids=true | all-gather | bytes 540672 | tf_op jit(solution)/shard_map/all_gather | solution.py:25
  166.2 1.3 fusion.15
  167.5 2.0 copy.26
  169.5 9.0 %gather_fusion.1 = bf16[2048,256]{1,0:T(8,128)(2,1)} fusion(bf16[4096,256]{1,0:T(8,128)(2,1)S(1)} %bitcast.50, s32[2048]{0:T(1024)S(1)} %broadcast_clamp_fusion.1), kind=kCustom, calls=%fused_computation.1 | custom fusion | bytes 2105344 | tf_op jit(solution)/shard_map/gather | solution.py:38
  178.5 1.4 reshape.188
  179.9 0.6 multiply_reduce_fusion
  180.7 28.9 %psum.7 = f32[512,4]{0,1:T(4,128)S(1)} all-reduce(f32[512,4]{0,1:T(4,128)S(1)} %copy.21), channel_id=1, replica_groups=mesh['dp'=32,'wide'=16] {'wide'}, use_global_device_ids=true, to_apply=%region_5.6 | all-reduce | flops 2048 | bytes 16384 | tf_op jit(solution)/shard_map/psum | solution.py:42
  209.6 0.9 copy.22
  210.5 2.1 fusion.16
  212.7 0.7 fusion.1
  213.4 0.8 copy.16
  214.3 0.6 compare_select_fusion.2
  214.9 91.9 %all-gather.2.cloned.1.call-done = bf16[512,4096]{1,0:T(8,128)(2,1)} async-done(((bf16[512,256]{1,0:T(8,128)(2,1)}), bf16[512,4096]{1,0:T(8,128)(2,1)}) %all-gather.2.cloned.1.call-update) | async-done | bytes 4194320 | tf_op jit(solution)/shard_map/all_gather | solution.py:47
  306.8 4.9 %convolution_convert_fusion = bf16[512,256]{1,0:T(8,128)(2,1)} fusion(bf16[512,4096]{1,0:T(8,128)(2,1)} %all-gather.2.cloned.1.call-done, bf16[256,4096]{1,0:T(8,128)(2,1)} %param.9, bf16[32,8,32,128]{3,2,1,0:T(8,128)(2,1)S(1)} %bitcast.52), kind=kOutput, calls=%fused_computation.6 | convolution fusion | flops 1074921472 | bytes 8650752 | tf_op jit(solution)/shard_map/dot_general | solution.py:48
  (41 shorter events, 2.6 us)
Async XLA Ops:
  7.2 159.0 %copy-start = (bf16[512,1024]{1,0:T(8,128)(2,1)S(1)}, bf16[512,1024]{1,0:T(8,128)(2,1)}, u32[]{:S(2)}) copy-start(bf16[512,1024]{1,0:T(8,128)(2,1)} %param.7) | copy-start | bytes 3145732
  7.2 34.4 %copy-start.1 = (bf16[512,256]{1,0:T(8,128)(2,1)S(1)}, bf16[512,256]{1,0:T(8,128)(2,1)}, u32[]{:S(2)}) copy-start(bf16[512,256]{1,0:T(8,128)(2,1)} %param.11) | copy-start | bytes 786436
  58.5 5.3 %copy-start.8 = (s32[2,32]{1,0:T(2,128)S(1)}, s32[2,32]{1,0:T(2,128)}, u32[]{:S(2)}) copy-start(s32[2,32]{1,0:T(2,128)} %param.10) | copy-start | bytes 772
  58.5 111.0 %all-to-all-start.1 = ((bf16[32,128,256]{2,1,0:T(8,128)(2,1)}), bf16[32,128,256]{2,1,0:T(8,128)(2,1)S(1)}, u32[]{:S(2)}, u32[]{:S(2)}) async-start(bf16[32,128,256]{2,1,0:T(8,128)(2,1)} %bitcast.53), calls=%async_computation.2 | async-start | bytes 4194304 | tf_op jit(solution)/shard_map/all_to_all | solution.py:37
  63.8 77.2 %reduce-scatter.2.cloned.1.call-start = ((), (), s32[]{:S(2)}) async-start(), calls=%async_computation.3 | async-start | bytes 557056 | tf_op jit(solution)/shard_map/reduce_scatter | solution.py:24
  63.8 2.2 copy-start.5
  64.2 1.3 copy-start.2
  68.5 238.3 %all-gather.2.cloned.1.call-start = ((), (), s32[]{:S(2)}) async-start(), calls=%async_computation.4 | async-start | bytes 4456448 | tf_op jit(solution)/shard_map/all_gather | solution.py:47
  178.5 1.4 copy-start.6
  178.5 31.1 %copy-start.7 = (s32[512,4]{0,1:T(4,128)S(1)}, s32[512,4]{0,1:T(4,128)}, u32[]{:S(2)}) copy-start(s32[512,4]{0,1:T(4,128)} %param.13) | copy-start | bytes 24580
  179.9 29.7 %copy-start.4 = (bf16[512,4,256]{2,1,0:T(4,128)(2,1)}, bf16[512,4,256]{2,1,0:T(4,128)(2,1)S(1)}, u32[]{:S(2)}) copy-start(bf16[512,4,256]{2,1,0:T(4,128)(2,1)S(1)} %reshape.188) | copy-start | bytes 3145732
  210.5 96.3 %copy-start.3 = (bf16[2,128,32,128]{3,2,1,0:T(8,128)(2,1)S(1)}, bf16[2,128,32,128]{3,2,1,0:T(8,128)(2,1)}, u32[]{:S(2)}) copy-start(bf16[2,128,32,128]{3,2,1,0:T(8,128)(2,1)} %copy-done.2) | copy-start | bytes 6291460
Sparse Core Ops, SparseCore 0:
  68.6 72.2 reduce-scatter.1
  213.6 93.1 all-gather.1
where the time goes:
time: 319 us
  waiting for transfers between devices  164 us (51%)
  blocking collectives  68.1 us (21%)
  local copies, waits for them, and re-layouts  43.3 us (14%)
  between operations  14.3 us (4%)
  other arithmetic  12.4 us (4%)
  matrix products  10.7 us (3%)
  starting transfers between devices  5.33 us (2%)
    all_gather x1, waiting for transfers between devices, local(): grad_full = lax.all_gather(grad_local, 'wide', axis=1, tiled=True)  91.9 us
    reduce_scatter x1, waiting for transfers between devices, local(): w_blk = lax.psum_scatter(w_part, 'wide', scatter_dimension=1, tiled=True)  72.4 us
    psum x1, blocking collectives, local(): score = lax.psum(partial_scores, 'wide') * scale  28.9 us
    all_gather x1, blocking collectives, local(): lax.all_gather(w_blk.astype(jnp.bfloat16), 'dp', axis=0, tiled=True)  24.5 us
    gather x1, local copies, waits for them, and re-layouts, local(): served = old_index[asked.reshape(-1)].reshape(n_dp, CAP, e_local)  16.9 us
    all_to_all x1, blocking collectives, local(): asked = lax.all_to_all(req.reshape(n_dp, CAP), 'dp', 0, 0, tiled=True)  14.8 us
    another operation x3, other arithmetic  9.41 us
    gather x1, local copies, waits for them, and re-layouts, local(): old_vec = back[slot].reshape(rows, K, e_local)  9 us
  transfers between devices with their start and end apart: 3, of which 2 were waited for; matrix products, arithmetic and copies ran while one was open for 3% of the time, Pallas kernels for 0%

commit v1 on v0

--- a/solution.py
+++ b/solution.py
@@ -44,7 +44,10 @@
     pair_loss = jax.nn.softplus(-sign * score)
     dscore = -sign * jax.nn.sigmoid(-sign * score)
     grad_local = (jnp.einsum("rk,rke->re", dscore, old_wide) * scale).astype(jnp.bfloat16)
-    grad_full = lax.all_gather(grad_local, "wide", axis=1, tiled=True)
+    grad_full = jnp.concatenate(
+        lax.all_to_all(jnp.stack([grad_local] * lax.axis_size("wide"), axis=0), "wide", 0, 0),
+        axis=1,
+    )
     trunk_grad = lax.dot_general(
         grad_full, masked, (((1,), (1,)), ((), ())), preferred_element_type=jnp.float32
     )

time: 319 us -> 418 us (1.31)
  waiting for transfers between devices: 164 us -> 251 us
  starting transfers between devices: 5.33 us -> 15.4 us
    all_to_all x0 -> x1, waiting for transfers between devices: none -> 179 us  [local(): lax.all_to_all(jnp.stack([grad_local] * lax.axis_size('wide'), axis=0), '...]
    all_gather x1 -> x0, waiting for transfers between devices: 91.9 us -> none  [local(): grad_full = lax.all_gather(grad_local, 'wide', axis=1, tiled=True)]
    all_to_all x0 -> x1, starting transfers between devices: none -> 10.1 us  [local(): lax.all_to_all(jnp.stack([grad_local] * lax.axis_size('wide'), axis=0), '...]
  transfers between devices with their start and end apart: 3 -> 3, of which waited for: 2 -> 2; matrix products, arithmetic and copies ran while one was open for 3% -> 2% of each run, Pallas kernels for 0% -> 0%
where the time goes in v1:
time: 418 us; the launch traced here: 417 us
  waiting for transfers between devices  251 us (60%)
  blocking collectives  68.1 us (16%)
  local copies, waits for them, and re-layouts  45.1 us (11%)
  starting transfers between devices  15.4 us (4%)
  other arithmetic  14.6 us (3%)
  between operations  14.3 us (3%)
  matrix products  8.82 us (2%)
    all_to_all x1, waiting for transfers between devices, local(): lax.all_to_all(jnp.stack([grad_local] * lax.axis_size('wide'), axis=0), '...  179 us
    reduce_scatter x1, waiting for transfers between devices, local(): w_blk = lax.psum_scatter(w_part, 'wide', scatter_dimension=1, tiled=True)  72.4 us
    psum x1, blocking collectives, local(): score = lax.psum(partial_scores, 'wide') * scale  28.9 us
    all_gather x1, blocking collectives, local(): lax.all_gather(w_blk.astype(jnp.bfloat16), 'dp', axis=0, tiled=True)  24.5 us
    gather x1, local copies, waits for them, and re-layouts, local(): served = old_index[asked.reshape(-1)].reshape(n_dp, CAP, e_local)  16.9 us
    all_to_all x1, blocking collectives, local(): asked = lax.all_to_all(req.reshape(n_dp, CAP), 'dp', 0, 0, tiled=True)  14.8 us
    all_to_all x1, starting transfers between devices, local(): lax.all_to_all(jnp.stack([grad_local] * lax.axis_size('wide'), axis=0), '...  10.1 us
    another operation x3, other arithmetic  9.41 us
  transfers between devices with their start and end apart: 3, of which 2 were waited for; matrix products, arithmetic and copies ran while one was open for 2% of the time, Pallas kernels for 0%

profile of v1, /device:TPU:2, one launch (start us, length us, event | category | flops | bytes accessed | tf_op | source)
XLA Modules:
  0.0 417.3 jit_solution(782373337876737471)
XLA Ops:
  7.2 0.9 copy.11
  8.7 9.1 %reduce-window.6 = s32[32,16,128]{2,1,0:T(8,128)S(1)} reduce-window(s32[32,16,128]{2,1,0:T(8,128)S(1)} %fusion.4, s32[]{:T(128)} %constant.20.clone.1), window={size=1x1x128 pad=0_0x0_0x127_0}, to_apply=%region_1.2 | reduce-window | flops 8323072 | bytes 524292 | tf_op jit(solution)/shard_map/reduce-window
  18.7 8.1 %scatter_custom_fusion = s32[4096]{0:T(1024)S(1)} fusion(s32[2048]{0:T(1024)S(1)} %bitcast.55, s32[2048]{0:T(1024)S(1)} %get-tuple-element.11, s32[]{:T(128)} %constant.20.clone.1), kind=kCustom, calls=%fused_computation.42 | custom fusion | bytes 16388 | tf_op jit(solution)/shard_map/scatter | solution.py:34
  26.7 14.8 %all_to_all.19 = s32[32,1,128]{2,1,0:T(1,128)S(1)} all-to-all(s32[32,1,128]{2,1,0:T(1,128)S(1)} %bitcast.52), channel_id=1, replica_groups=mesh['dp'=32,'wide'=16] {'dp'}, dimensions={0} | all-to-all | bytes 32768 | tf_op jit(solution)/shard_map/all_to_all | solution.py:35
  41.6 16.9 %gather_fusion = bf16[4096,256]{1,0:T(8,128)(2,1)} fusion(bf16[512,256]{1,0:T(8,128)(2,1)S(1)} %copy-done.1, s32[4096]{0:T(1024)S(1)} %broadcast_clamp_fusion), kind=kCustom, calls=%fused_computation | custom fusion | bytes 4210688 | tf_op jit(solution)/shard_map/gather | solution.py:36
  58.5 5.2 %all-to-all-start.1 = ((bf16[32,128,256]{2,1,0:T(8,128)(2,1)}), bf16[32,128,256]{2,1,0:T(8,128)(2,1)S(1)}, u32[]{:S(2)}, u32[]{:S(2)}) async-start(bf16[32,128,256]{2,1,0:T(8,128)(2,1)} %bitcast.48), calls=%async_computation.2 | async-start | bytes 4194304 | tf_op jit(solution)/shard_map/all_to_all | solution.py:37
  64.2 1.4 copy-done.2
  66.1 2.4 fusion
  68.5 72.4 %reduce-scatter.2.cloned.1.call-done = f32[32,256]{1,0:T(8,128)} async-done(((f32[32,4096]{1,0:T(8,128)}), f32[32,256]{1,0:T(8,128)}) %reduce-scatter.2.cloned.1.call-update) | async-done | bytes 32784 | tf_op jit(solution)/shard_map/reduce_scatter | solution.py:24
  140.9 0.8 convert_element_type.28
  141.7 24.5 %all_gather.3 = bf16[1024,256]{1,0:T(8,128)(2,1)S(1)} all-gather(bf16[32,256]{1,0:T(8,128)(2,1)S(1)} %convert_element_type.28), channel_id=1, replica_groups=mesh['dp'=32,'wide'=16] {'dp'}, dimensions={0}, use_global_device_ids=true | all-gather | bytes 540672 | tf_op jit(solution)/shard_map/all_gather | solution.py:25
  166.2 1.3 fusion.13
  167.5 2.0 copy.28
  169.5 9.0 %gather_fusion.1 = bf16[2048,256]{1,0:T(8,128)(2,1)} fusion(bf16[4096,256]{1,0:T(8,128)(2,1)S(1)} %bitcast.45, s32[2048]{0:T(1024)S(1)} %broadcast_clamp_fusion.1), kind=kCustom, calls=%fused_computation.1 | custom fusion | bytes 2105344 | tf_op jit(solution)/shard_map/gather | solution.py:38
  178.5 1.4 reshape.196
  179.9 0.6 multiply_reduce_fusion.1
  180.7 28.9 %psum.7 = f32[512,4]{0,1:T(4,128)S(1)} all-reduce(f32[512,4]{0,1:T(4,128)S(1)} %copy.21), channel_id=1, replica_groups=mesh['dp'=32,'wide'=16] {'wide'}, use_global_device_ids=true, to_apply=%region_5.6 | all-reduce | flops 2048 | bytes 16384 | tf_op jit(solution)/shard_map/psum | solution.py:42
  209.6 0.6 divide_multiply_fusion
  210.3 2.9 multiply_reduce_fusion
  213.5 2.4 stack.2
  215.8 10.1 %all-to-all-start.2 = ((bf16[16,512,256]{1,2,0:T(8,128)(2,1)}), bf16[16,512,256]{1,2,0:T(8,128)(2,1)}, u32[]{:S(2)}, u32[]{:S(2)}) async-start(bf16[16,512,256]{1,2,0:T(8,128)(2,1)} %stack.2), calls=%async_computation.3 | async-start | bytes 8388608 | tf_op jit(solution)/shard_map/all_to_all | solution.py:48
  226.0 0.8 copy.16
  226.8 178.5 %all-to-all-done.2 = bf16[16,512,256]{1,2,0:T(8,128)(2,1)} async-done(((bf16[16,512,256]{1,2,0:T(8,128)(2,1)}), bf16[16,512,256]{1,2,0:T(8,128)(2,1)}, u32[]{:S(2)}, u32[]{:S(2)}) %all-to-all-start.2) | async-done | bytes 4194336 | tf_op jit(solution)/shard_map/all_to_all | solution.py:48
  405.3 5.1 %convolution_convert_fusion = bf16[512,256]{1,0:T(8,128)(2,1)} fusion(bf16[512,4096]{0,1:T(8,128)(2,1)} %bitcast.13, bf16[256,4096]{1,0:T(8,128)(2,1)} %param.9, bf16[32,8,32,128]{3,2,1,0:T(8,128)(2,1)S(1)} %bitcast.47), kind=kOutput, calls=%fused_computation.7 | convolution fusion | flops 1074921472 | bytes 8650752 | tf_op jit(solution)/shard_map/dot_general | solution.py:51
  (39 shorter events, 2.8 us)
Async XLA Ops:
  7.2 159.0 %copy-start = (bf16[512,1024]{1,0:T(8,128)(2,1)S(1)}, bf16[512,1024]{1,0:T(8,128)(2,1)}, u32[]{:S(2)}) copy-start(bf16[512,1024]{1,0:T(8,128)(2,1)} %param.7) | copy-start | bytes 3145732
  7.2 34.4 %copy-start.1 = (bf16[512,256]{1,0:T(8,128)(2,1)S(1)}, bf16[512,256]{1,0:T(8,128)(2,1)}, u32[]{:S(2)}) copy-start(bf16[512,256]{1,0:T(8,128)(2,1)} %param.11) | copy-start | bytes 786436
  58.5 5.3 %copy-start.7 = (s32[2,32]{1,0:T(2,128)S(1)}, s32[2,32]{1,0:T(2,128)}, u32[]{:S(2)}) copy-start(s32[2,32]{1,0:T(2,128)} %param.10) | copy-start | bytes 772
  58.5 111.0 %all-to-all-start.1 = ((bf16[32,128,256]{2,1,0:T(8,128)(2,1)}), bf16[32,128,256]{2,1,0:T(8,128)(2,1)S(1)}, u32[]{:S(2)}, u32[]{:S(2)}) async-start(bf16[32,128,256]{2,1,0:T(8,128)(2,1)} %bitcast.48), calls=%async_computation.2 | async-start | bytes 4194304 | tf_op jit(solution)/shard_map/all_to_all | solution.py:37
  63.8 77.2 %reduce-scatter.2.cloned.1.call-start = ((), (), s32[]{:S(2)}) async-start(), calls=%async_computation.4 | async-start | bytes 557056 | tf_op jit(solution)/shard_map/reduce_scatter | solution.py:24
  63.8 2.2 copy-start.4
  64.2 1.4 copy-start.2
  178.5 1.4 copy-start.5
  178.5 31.1 %copy-start.6 = (s32[512,4]{0,1:T(4,128)S(1)}, s32[512,4]{0,1:T(4,128)}, u32[]{:S(2)}) copy-start(s32[512,4]{0,1:T(4,128)} %param.13) | copy-start | bytes 24580
  215.8 189.5 %copy-start.3 = (bf16[2,128,32,128]{3,2,1,0:T(8,128)(2,1)S(1)}, bf16[2,128,32,128]{3,2,1,0:T(8,128)(2,1)}, u32[]{:S(2)}) copy-start(bf16[2,128,32,128]{3,2,1,0:T(8,128)(2,1)} %copy-done.2) | copy-start | bytes 6291460
  215.8 189.5 %all-to-all-start.2 = ((bf16[16,512,256]{1,2,0:T(8,128)(2,1)}), bf16[16,512,256]{1,2,0:T(8,128)(2,1)}, u32[]{:S(2)}, u32[]{:S(2)}) async-start(bf16[16,512,256]{1,2,0:T(8,128)(2,1)} %stack.2), calls=%async_computation.3 | async-start | bytes 8388608 | tf_op jit(solution)/shard_map/all_to_all | solution.py:48
Sparse Core Ops, SparseCore 0:
  68.6 72.2 reduce-scatter.1
